TPU v7x, 256 devices: a whole 4x4x8 slice. The times are simulated.
256 devices in a mesh: dp: 32 (over x_lo, z, core), blk: 8 (over y, x_hi).
Axes of the slice: x: 4 (x_hi: 2, x_lo: 2; x = x_hi * 2 + x_lo), y: 4, z: 8, core: 2. Of those that a mesh axis runs over, the one named last changes fastest.
Arguments:
- inputs: bfloat16 [8, 16384, 4096], P('blk', 'dp'), may hold values from -6 to 6
- out_grads: bfloat16 [8, 16384, 4096], P('blk', 'dp'), may hold values from -8 to 8
- test_matrix: bfloat16 [8, 4096, 256], P('blk'), may hold values from -6 to 6
- momentum: bfloat16 [8, 4096, 4096], P(None, 'blk', 'dp'), may hold values from -6 to 6
Outputs:
- update: bfloat16 [8, 4096, 4096], P(None, 'blk', 'dp')
All inputs are finite; a program needn't handle non-finite values.
Results may differ from a plain program's by a relative error of at most 0.0035.
Values may be sent and summed in bfloat16 or wider, within the bound.
No kernel may reach another device: no remote copies, remote signals or barrier semaphores. Data moves between devices by JAX's collectives and lax.ppermute only.
A program may use at most 128 MiB of HBM per device.

v0:
```python
import jax
import jax.numpy as jnp
from jax import lax
from jax.sharding import Mesh
from jax.sharding import PartitionSpec as P

DP = ("dp_0", "dp_1", "dp_2")


def filled_up(lines, devices):
    spare = -len(lines) % devices
    return jnp.pad(lines, [(0, spare)] + [(0, 0)] * (lines.ndim - 1))


def copy_for_each(x, axis):
    devices = lax.axis_size(axis)
    return lax.all_to_all(jnp.broadcast_to(x[None], (devices, *x.shape)), axis, 0, 0, tiled=True)


def in_order(blocks, dim):
    blocks = jnp.moveaxis(blocks, 0, dim)
    lengths = blocks.shape
    return blocks.reshape(*lengths[:dim], lengths[dim] * lengths[dim + 1], *lengths[dim + 2 :])


def whole_of(x, axes, dim):
    far, near = axes
    first = copy_for_each(x, far)
    blocks = jnp.swapaxes(copy_for_each(first, near), 0, 1)
    return in_order(blocks.reshape(-1, *x.shape), dim)


def in_blocks(x, dim, devices):
    lengths = x.shape
    blocks = x.reshape(*lengths[:dim], devices, lengths[dim] // devices, *lengths[dim + 1 :])
    return jnp.moveaxis(blocks, dim, 0)


def sum_at_owner(x, axis, dim):
    blocks = in_blocks(x, dim, lax.axis_size(axis))
    arrived = lax.all_to_all(blocks, axis, split_axis=0, concat_axis=0, tiled=True)
    return arrived.sum(axis=0)


def sum_by_axis(x, axes, dim):
    far, near = axes
    blocks = in_blocks(x, dim, lax.axis_size(far))
    nearer = sum_at_owner(blocks, near, dim + 1)
    arrived = lax.all_to_all(nearer, far, split_axis=0, concat_axis=0, tiled=True)
    return arrived.sum(axis=0)


def total_of(x, axes):
    lines = x.reshape(-1, x.shape[-1])
    padded = filled_up(lines, lax.axis_size(axes[0]) * lax.axis_size(axes[1]))
    whole = whole_of(sum_by_axis(padded, axes, 0), axes, 0)
    return lax.slice_in_dim(whole, 0, len(lines)).reshape(x.shape)


def collect(x, axis, dim):
    blocks = copy_for_each(x, axis)
    return in_order(blocks, dim)


def total_of_2(x, axes):
    lines = x.reshape(-1, x.shape[-1])
    own = sum_at_owner(filled_up(lines, lax.axis_size(axes)), axes, 0)
    whole = collect(own, axes, 0)
    return whole[: len(lines)].reshape(x.shape)


def inner_gram(columns):
    return lax.dot_general(
        columns, columns, (((0,), (0,)), ((), ())), precision=lax.Precision.HIGHEST
    )


def cholesky_pass(columns, gram_matrix):
    lower_factor = jnp.linalg.cholesky(gram_matrix)
    return lax.linalg.triangular_solve(
        lower_factor, columns, left_side=False, lower=True, transpose_a=True
    )


def shards(inputs, out_grads, test_matrix, momentum):
    features = inputs[0]
    errors = out_grads[0]
    probes = test_matrix[0]
    replicas = lax.axis_size(DP)
    scale = 1.0 / (features.shape[1] * features.shape[0] * replicas)
    projected = jnp.dot(features, probes, preferred_element_type=jnp.float32).astype(jnp.bfloat16)
    token_gram = lax.dot_general(
        errors, errors, (((1,), (1,)), ((), ())), preferred_element_type=jnp.float32
    ).astype(jnp.bfloat16)
    mixed_rows = jnp.dot(token_gram, projected, preferred_element_type=jnp.float32).astype(
        jnp.bfloat16
    )
    sketch_term = (
        lax.dot_general(
            features, mixed_rows, (((0,), (0,)), ((), ())), preferred_element_type=jnp.float32
        )
        * scale
    )
    sketch = total_of(sketch_term, (("dp_0", "dp_1"), "dp_2"))
    basis = cholesky_pass(sketch, inner_gram(sketch)).astype(jnp.bfloat16)
    reduced = jnp.dot(features, basis, preferred_element_type=jnp.float32).astype(jnp.bfloat16)
    shaped = jnp.dot(token_gram, reduced, preferred_element_type=jnp.float32).astype(jnp.bfloat16)
    core_term = (
        lax.dot_general(
            reduced, shaped, (((0,), (0,)), ((), ())), preferred_element_type=jnp.float32
        )
        * scale
    )
    core_matrix = total_of_2(core_term, DP)
    shifted = core_matrix + jnp.eye(core_matrix.shape[0], dtype=jnp.float32)
    lower_factor = jnp.linalg.cholesky(shifted)
    half_solved = lax.linalg.triangular_solve(lower_factor, core_matrix, left_side=True, lower=True)
    factor = lax.linalg.triangular_solve(
        lower_factor, half_solved, left_side=True, lower=True, transpose_a=True
    )
    columns = lax.all_to_all(momentum, "blk", split_axis=0, concat_axis=1, tiled=True)[0]
    coeffs = lax.dot_general(
        basis, columns, (((0,), (0,)), ((), ())), preferred_element_type=jnp.float32
    )
    scaled = jnp.dot(factor, coeffs, precision=lax.Precision.HIGHEST).astype(jnp.bfloat16)
    fresh = (
        columns.astype(jnp.float32) - jnp.dot(basis, scaled, preferred_element_type=jnp.float32)
    ).astype(jnp.bfloat16)
    return lax.all_to_all(fresh[None], "blk", split_axis=1, concat_axis=0, tiled=True)


def solution(mesh):
    torus = Mesh(mesh.devices.reshape(2, 8, 2, mesh.shape["blk"]), ("dp_0", "dp_1", "dp_2", "blk"))
    in_specs = (P("blk", DP, None), P("blk", DP, None), P("blk", None, None), P(None, "blk", DP))
    out_specs = P(None, "blk", DP)
    return jax.shard_map(
        shards, mesh=torus, in_specs=in_specs, out_specs=out_specs, check_vma=False
    )
```

profile of v0, /device:TPU:1, one launch (start us, length us, event | category | flops | bytes accessed | tf_op | source)
XLA Modules:
  0.0 433.6 jit_solution(7566562634158218286)
XLA Ops:
  0.0 6.0 %fusion.16 = bf16[512,512]{1,0:T(8,128)(2,1)S(1)} fusion(bf16[1,512,4096]{2,1,0:T(8,128)(2,1)} %param.6), kind=kOutput, calls=%fused_computation.26 | convolution fusion | flops 2147745792 | bytes 4718592 | tf_op jit(solution)/shard_map/dot_general | solution.py:92
  6.0 1.3 fusion.19
  7.3 5.9 %fusion = f32[4096,256]{0,1:T(8,128)} fusion(bf16[1,512,4096]{2,1,0:T(8,128)(2,1)} %param.5, bf16[512,512]{1,0:T(8,128)(2,1)S(1)} %fusion.16, bf16[512,256]{1,0:T(8,128)(2,1)S(1)} %fusion.19), kind=kOutput, calls=%fused_computation.5 | convolution fusion | flops 1209139200 | bytes 9175040 | tf_op jit(solution)/shard_map/dot_general | solution.py:99
  13.2 6.6 %reshape_reshape.6 = f32[16,2,128,256]{2,1,0,3:T(2,128)} reshape(f32[4096,256]{0,1:T(8,128)} %fusion) | data formatting | bytes 8388608 | tf_op jit(solution)/shard_map/reshape;reshape | solution.py:35
  19.8 4.5 %copy.56 = f32[16,2,128,256]{2,0,3,1:T(8,128)} copy(f32[16,2,128,256]{2,1,0,3:T(2,128)} %reshape_reshape.6) | data formatting | bytes 8388608 | tf_op jit(solution)/shard_map/reshape;reshape | solution.py:35
  24.2 8.8 %all-to-all-start.1 = ((f32[2,16,128,256]{2,1,3,0:T(8,128)}), f32[2,16,128,256]{2,1,3,0:T(8,128)}, u32[]{:S(2)}, u32[]{:S(2)}) async-start(f32[2,16,128,256]{2,1,3,0:T(8,128)} %bitcast.138), calls=%async_computation.1 | async-start | bytes 8388608 | tf_op jit(solution)/shard_map/all_to_all | solution.py:41
  33.1 4.1 all-to-all-done.1
  37.2 2.7 reduce_sum.27
  39.9 0.7 copy.30
  40.6 54.2 %all_to_all.54 = f32[16,128,256]{1,2,0:T(8,128)S(1)} all-to-all(f32[16,128,256]{1,2,0:T(8,128)S(1)} %copy.30), channel_id=1, replica_groups=mesh['dp_0'=2,'dp_1'=8,'dp_2'=2,'blk'=8] {'dp_0','dp_1'}, dimensions={0} | all-to-all | bytes 4194304 | tf_op jit(solution)/shard_map/all_to_all | solution.py:49
  95.1 1.6 broadcast_in_dim.8
  96.6 7.1 %all-to-all-start.3 = ((f32[16,128,256]{2,1,0:T(8,128)}), f32[16,128,256]{2,1,0:T(8,128)S(1)}, u32[]{:S(2)}, u32[]{:S(2)}) async-start(f32[16,128,256]{2,1,0:T(8,128)} %broadcast_in_dim.8), calls=%async_computation.3 | async-start | bytes 4194304 | tf_op jit(solution)/shard_map/all_to_all | solution.py:17
  103.7 47.7 %all-to-all-done.3 = f32[16,128,256]{2,1,0:T(8,128)S(1)} async-done(((f32[16,128,256]{2,1,0:T(8,128)}), f32[16,128,256]{2,1,0:T(8,128)S(1)}, u32[]{:S(2)}, u32[]{:S(2)}) %all-to-all-start.3) | async-done | bytes 2097184 | tf_op jit(solution)/shard_map/all_to_all | solution.py:17
  151.4 0.5 broadcast_in_dim.10
  151.9 8.8 %all_to_all.51 = f32[2,16,128,256]{3,2,1,0:T(8,128)S(1)} all-to-all(f32[2,16,128,256]{3,2,1,0:T(8,128)S(1)} %broadcast_in_dim.10), channel_id=1, replica_groups=mesh['dp_0'=2,'dp_1'=8,'dp_2'=2,'blk'=8] {'dp_2'}, dimensions={0} | all-to-all | bytes 8388608 | tf_op jit(solution)/shard_map/all_to_all | solution.py:17
  160.7 1.9 copy-done.2
  162.6 6.8 %fusion.28 = f32[256,256]{1,0:T(8,128)S(1)} fusion(f32[2,16,128,256]{3,2,1,0:T(8,128)S(1)} %all_to_all.51), kind=kOutput, calls=%fused_computation.32 | convolution fusion | flops 3221225472 | bytes 4456448 | tf_op jit(solution)/shard_map/dot_general | solution.py:73
  169.6 11.7 %cholesky.130 = f32[128,128]{1,0:T(8,128)S(1)} custom-call(f32[128,128]{1,0:T(8,128)S(1)} %cholesky.194), custom_call_target="Cholesky" | custom-call | tf_op jit(solution)/shard_map/jit(cholesky)/cholesky | solution.py:79
  181.4 10.2 %custom-call.19 = f32[1,128,128]{1,2,0:T(8,128)S(1)} custom-call(f32[1,128,128]{2,1,0:T(8,128)S(1)} %get-tuple-element.49), custom_call_target="InvertDiagBlocksLowerTriangular" | custom-call | tf_op jit(solution)/shard_map/jit(cholesky)/cholesky | solution.py:79
  192.1 11.7 %cholesky.147 = f32[128,128]{1,0:T(8,128)S(1)} custom-call(f32[128,128]{1,0:T(8,128)S(1)} %convolution_subtract_fusion.5), custom_call_target="Cholesky" | custom-call | tf_op jit(solution)/shard_map/jit(cholesky)/cholesky | solution.py:79
  203.8 0.7 compare_reduce_fusion.2
  206.0 4.1 while.2
  206.0 0.6 fusion.84
  206.6 1.4 bitcast_dynamic-update-slice_fusion.4
  208.0 0.6 fusion.84
  208.7 1.4 bitcast_dynamic-update-slice_fusion.4
  210.1 19.8 %custom-call.16 = f32[2,128,128]{1,2,0:T(8,128)S(1)} custom-call(f32[2,128,128]{2,1,0:T(8,128)S(1)} %get-tuple-element.13), custom_call_target="InvertDiagBlocksLowerTriangular" | custom-call | tf_op jit(solution)/shard_map/triangular_solve | solution.py:80
  229.9 2.5 copy.33
  232.5 2.0 fusion.61
  234.5 3.5 convolution_subtract_fusion.1
  238.1 2.0 convolution_convert_fusion
  240.1 1.0 copy-done.5
  241.1 1.3 fusion.24
  242.4 0.6 fusion.34
  243.0 17.9 %all_to_all.52 = f32[32,8,256]{2,1,0:T(8,128)S(1)} all-to-all(f32[32,8,256]{2,1,0:T(8,128)S(1)} %fusion.34), channel_id=1, replica_groups=mesh['dp_0'=2,'dp_1'=8,'dp_2'=2,'blk'=8] {'dp_0','dp_1','dp_2'}, dimensions={0} | all-to-all | bytes 524288 | tf_op jit(solution)/shard_map/all_to_all | solution.py:41
  260.9 6.4 %all-to-all-start = ((bf16[8,512,128]{2,1,0:T(8,128)(2,1)}), bf16[8,512,128]{2,1,0:T(8,128)(2,1)S(1)}, u32[]{:S(2)}, u32[]{:S(2)}) async-start(bf16[8,512,128]{2,1,0:T(8,128)(2,1)} %param.8), calls=%async_computation | async-start | bytes 2097152 | tf_op jit(solution)/shard_map/all_to_all | solution.py:121
  267.3 15.1 %all-to-all-done = bf16[8,512,128]{2,1,0:T(8,128)(2,1)S(1)} async-done(((bf16[8,512,128]{2,1,0:T(8,128)(2,1)}), bf16[8,512,128]{2,1,0:T(8,128)(2,1)S(1)}, u32[]{:S(2)}, u32[]{:S(2)}) %all-to-all-start) | async-done | bytes 1048608 | tf_op jit(solution)/shard_map/all_to_all | solution.py:121
  282.4 0.7 broadcast_in_dim.11
  283.2 6.8 %all-to-all-start.6 = ((f32[32,8,256]{2,1,0:T(8,128)}), f32[32,8,256]{2,1,0:T(8,128)S(1)}, u32[]{:S(2)}, u32[]{:S(2)}) async-start(f32[32,8,256]{2,1,0:T(8,128)} %broadcast_in_dim.11), calls=%async_computation.6 | async-start | bytes 524288 | tf_op jit(solution)/shard_map/all_to_all | solution.py:17
  290.0 1.9 fusion.35
  291.9 10.0 %all-to-all-done.6 = f32[32,8,256]{2,1,0:T(8,128)S(1)} async-done(((f32[32,8,256]{2,1,0:T(8,128)}), f32[32,8,256]{2,1,0:T(8,128)S(1)}, u32[]{:S(2)}, u32[]{:S(2)}) %all-to-all-start.6) | async-done | bytes 262176 | tf_op jit(solution)/shard_map/all_to_all | solution.py:17
  302.3 11.7 %cholesky.164 = f32[128,128]{1,0:T(8,128)S(1)} custom-call(f32[128,128]{1,0:T(8,128)S(1)} %cholesky.197), custom_call_target="Cholesky" | custom-call | tf_op jit(solution)/shard_map/jit(cholesky)/cholesky | solution.py:116
  314.1 9.8 %custom-call.20 = f32[1,128,128]{1,2,0:T(8,128)S(1)} custom-call(f32[1,128,128]{2,1,0:T(8,128)S(1)} %get-tuple-element.45), custom_call_target="InvertDiagBlocksLowerTriangular" | custom-call | tf_op jit(solution)/shard_map/jit(cholesky)/cholesky | solution.py:116
  324.4 11.7 %cholesky.181 = f32[128,128]{1,0:T(8,128)S(1)} custom-call(f32[128,128]{1,0:T(8,128)S(1)} %convolution_subtract_fusion.4), custom_call_target="Cholesky" | custom-call | tf_op jit(solution)/shard_map/jit(cholesky)/cholesky | solution.py:116
  336.1 0.7 compare_reduce_fusion
  336.8 0.6 compare_reduce_fusion.1
  338.9 4.1 while.3
  338.9 0.6 fusion.85
  339.5 1.4 bitcast_dynamic-update-slice_fusion.5
  340.9 0.6 fusion.85
  341.5 1.4 bitcast_dynamic-update-slice_fusion.5
  343.0 19.9 %custom-call.17 = f32[2,128,128]{1,2,0:T(8,128)S(1)} custom-call(f32[2,128,128]{2,1,0:T(8,128)S(1)} %get-tuple-element.21), custom_call_target="InvertDiagBlocksLowerTriangular" | custom-call | tf_op jit(solution)/shard_map/triangular_solve | solution.py:118
  362.9 0.3 fusion.41
  363.5 0.3 fusion.51
  364.1 0.3 convolution_subtract_fusion.2
  364.6 0.4 convolution_convert_fusion.3
  365.0 2.0 fusion.2
  367.0 16.7 %copy.57 = bf16[1,4096,128]{2,0,1:T(2,128)(2,1)S(1)} copy(bf16[1,4096,128]{2,1,0:T(8,128)(2,1)S(1)} %fusion.2) | data formatting | bytes 2097152 | tf_op jit(solution)/shard_map/broadcast_in_dim | solution.py:129
  383.8 0.5 broadcast.130
  384.3 22.4 %reduce.8 = bf16[4096,128]{1,0:T(8,128)(2,1)S(1)} reduce(bf16[4096,1,128]{2,1,0:T(2,128)(2,1)S(1)} %bitcast.142, bf16[]{:T(256)} %broadcast.130), dimensions={1}, to_apply=%bitcast.125.reduce_sub_computation | reduce | bytes 2097154
  406.7 1.1 reshape.82
  407.8 19.2 %all_to_all.53 = bf16[8,2,32768]{2,1,0:T(2,128)(2,1)S(1)} all-to-all(bf16[8,2,32768]{2,1,0:T(2,128)(2,1)} %reshape.82), channel_id=1, replica_groups=mesh['dp_0'=2,'dp_1'=8,'dp_2'=2,'blk'=8] {'blk'}, dimensions={0} | all-to-all | bytes 2097152 | tf_op jit(solution)/shard_map/all_to_all | solution.py:129
  427.0 3.5 reshape.83
  430.5 2.7 copy.43
  (48 shorter events, 2.9 us)
Async XLA Ops:
  0.0 6.0 %copy-start = (bf16[1,4096,256]{2,1,0:T(8,128)(2,1)S(1)}, bf16[1,4096,256]{2,1,0:T(8,128)(2,1)}, u32[]{:S(2)}) copy-start(bf16[1,4096,256]{2,1,0:T(8,128)(2,1)} %param.7) | copy-start | bytes 6291460
  0.0 6.0 %copy-start.3 = (bf16[1,512,4096]{2,1,0:T(8,128)(2,1)S(1)}, bf16[1,512,4096]{2,1,0:T(8,128)(2,1)}, u32[]{:S(2)}) copy-start(bf16[1,512,4096]{2,1,0:T(8,128)(2,1)} %param.5) | copy-start | bytes 12582916
  24.2 13.0 %all-to-all-start.1 = ((f32[2,16,128,256]{2,1,3,0:T(8,128)}), f32[2,16,128,256]{2,1,3,0:T(8,128)}, u32[]{:S(2)}, u32[]{:S(2)}) async-start(f32[2,16,128,256]{2,1,3,0:T(8,128)} %bitcast.138), calls=%async_computation.1 | async-start | bytes 8388608 | tf_op jit(solution)/shard_map/all_to_all | solution.py:41
  96.6 54.8 %all-to-all-start.3 = ((f32[16,128,256]{2,1,0:T(8,128)}), f32[16,128,256]{2,1,0:T(8,128)S(1)}, u32[]{:S(2)}, u32[]{:S(2)}) async-start(f32[16,128,256]{2,1,0:T(8,128)} %broadcast_in_dim.8), calls=%async_computation.3 | async-start | bytes 4194304 | tf_op jit(solution)/shard_map/all_to_all | solution.py:17
  160.7 1.9 copy-start.2
  234.5 5.6 %copy-start.7 = (bf16[4096,128]{0,1:T(8,128)(2,1)}, bf16[4096,128]{0,1:T(8,128)(2,1)S(1)}, u32[]{:S(2)}) copy-start(bf16[4096,128]{0,1:T(8,128)(2,1)S(1)} %get-tuple-element.52) | copy-start | bytes 3145732
  234.5 6.6 %copy-start.4 = (bf16[1,512,4096]{2,1,0:T(8,128)(2,1)S(1)}, bf16[1,512,4096]{2,1,0:T(8,128)(2,1)}, u32[]{:S(2)}) copy-start(bf16[1,512,4096]{2,1,0:T(8,128)(2,1)} %param.5) | copy-start | bytes 12582916
  240.1 1.0 copy-start.5
  242.4 47.6 %copy-start.6 = (bf16[4096,128]{0,1:T(8,128)(2,1)S(1)}, bf16[4096,128]{0,1:T(8,128)(2,1)}, u32[]{:S(2)}) copy-start(bf16[4096,128]{0,1:T(8,128)(2,1)} %copy-done.5) | copy-start | bytes 3145732
  260.9 21.5 %all-to-all-start = ((bf16[8,512,128]{2,1,0:T(8,128)(2,1)}), bf16[8,512,128]{2,1,0:T(8,128)(2,1)S(1)}, u32[]{:S(2)}, u32[]{:S(2)}) async-start(bf16[8,512,128]{2,1,0:T(8,128)(2,1)} %param.8), calls=%async_computation | async-start | bytes 2097152 | tf_op jit(solution)/shard_map/all_to_all | solution.py:121
  283.2 18.8 %all-to-all-start.6 = ((f32[32,8,256]{2,1,0:T(8,128)}), f32[32,8,256]{2,1,0:T(8,128)S(1)}, u32[]{:S(2)}, u32[]{:S(2)}) async-start(f32[32,8,256]{2,1,0:T(8,128)} %broadcast_in_dim.11), calls=%async_computation.6 | async-start | bytes 524288 | tf_op jit(solution)/shard_map/all_to_all | solution.py:17
  406.7 26.5 %copy-start.1 = (bf16[1,4096,256]{2,1,0:T(8,128)(2,1)S(1)}, bf16[1,4096,256]{2,1,0:T(8,128)(2,1)}, u32[]{:S(2)}) copy-start(bf16[1,4096,256]{2,1,0:T(8,128)(2,1)} %param.7) | copy-start | bytes 6291460
where the time goes:
time: 441 us; the launch traced here: 434 us
  other arithmetic  134 us (30%)
  blocking collectives  100 us (23%)
  waiting for transfers between devices  76.9 us (17%)
  local copies, waits for them, and re-layouts  53.2 us (12%)
  matrix products  36.3 us (8%)
  starting transfers between devices  29.1 us (7%)
    all_to_all x2, waiting for transfers between devices, copy_for_each(): lax.all_to_all(jnp.broadcast_to(x[None], (devices, *x.shape)), axis, 0, 0...  57.7 us
    all_to_all x1, blocking collectives, sum_by_axis(): lax.all_to_all(nearer, far, split_axis=0, concat_axis=0, tiled=True)  54.2 us
    another operation x7, other arithmetic, shards(): lower_factor = jnp.linalg.cholesky(shifted)  34.7 us
    another operation x6, other arithmetic, cholesky_pass(): lower_factor = jnp.linalg.cholesky(gram_matrix)  34.4 us
    unnamed x1, other arithmetic  22.4 us
    another operation x2, other arithmetic, shards(): lax.linalg.triangular_solve(lower_factor, half_solved, left_side=True, lo...  20 us
    another operation x3, other arithmetic, cholesky_pass(): lax.linalg.triangular_solve(lower_factor, columns, left_side=False, lower...  19.9 us
    all_to_all x1, blocking collectives, shards(): lax.all_to_all(fresh[None], 'blk', split_axis=1, concat_axis=0, tiled=True)  19.2 us
  transfers between devices with their start and end apart: 4, of which 4 were waited for; matrix products, arithmetic and copies ran while one was open for 0% of the time, Pallas kernels for 0%

commit v1 on v0

--- a/solution.py
+++ b/solution.py
@@ -126,7 +126,12 @@
     fresh = (
         columns.astype(jnp.float32) - jnp.dot(basis, scaled, preferred_element_type=jnp.float32)
     ).astype(jnp.bfloat16)
-    return lax.all_to_all(fresh[None], "blk", split_axis=1, concat_axis=0, tiled=True)
+    return jnp.concatenate(
+        lax.all_to_all(
+            jnp.stack(jnp.split(fresh[None], lax.axis_size("blk"), axis=1)), "blk", 0, 0
+        ),
+        axis=0,
+    )
 
 
 def solution(mesh):

time: 441 us -> 394 us (0.89)
  local copies, waits for them, and re-layouts: 53.2 us -> 29.6 us
  other arithmetic: 134 us -> 112 us
    unnamed x1 -> x0, other arithmetic: 22.4 us -> none
    broadcast_in_dim x1 -> x0, local copies, waits for them, and re-layouts: 16.7 us -> none  [shards(): fresh[None]]
    unnamed x22 -> x30, local copies, waits for them, and re-layouts: 10.7 us -> 4.04 us
  transfers between devices with their start and end apart: 4 -> 4, of which waited for: 4 -> 4; matrix products, arithmetic and copies ran while one was open for 0% -> 1% of each run, Pallas kernels for 0% -> 0%
where the time goes in v1:
time: 394 us; the launch traced here: 387 us
  other arithmetic  112 us (28%)
  blocking collectives  99.1 us (25%)
  waiting for transfers between devices  76.9 us (20%)
  matrix products  36.8 us (9%)
  local copies, waits for them, and re-layouts  29.6 us (8%)
  starting transfers between devices  29 us (7%)
    all_to_all x2, waiting for transfers between devices, copy_for_each(): lax.all_to_all(jnp.broadcast_to(x[None], (devices, *x.shape)), axis, 0, 0...  57.7 us
    all_to_all x1, blocking collectives, sum_by_axis(): lax.all_to_all(nearer, far, split_axis=0, concat_axis=0, tiled=True)  54.2 us
    another operation x7, other arithmetic, shards(): lower_factor = jnp.linalg.cholesky(shifted)  34.6 us
    another operation x6, other arithmetic, cholesky_pass(): lower_factor = jnp.linalg.cholesky(gram_matrix)  34.2 us
    another operation x3, other arithmetic, cholesky_pass(): lax.linalg.triangular_solve(lower_factor, columns, left_side=False, lower...  20.1 us
    another operation x2, other arithmetic, shards(): lax.linalg.triangular_solve(lower_factor, half_solved, left_side=True, lo...  19.9 us
    all_to_all x1, blocking collectives, shards(): lax.all_to_all(jnp.stack(jnp.split(fresh[None], lax.axis_size('blk'), axi...  18.1 us
    all_to_all x1, blocking collectives, sum_at_owner(): lax.all_to_all(blocks, axis, split_axis=0, concat_axis=0, tiled=True)  17.9 us
  transfers between devices with their start and end apart: 4, of which 4 were waited for; matrix products, arithmetic and copies ran while one was open for 1% of the time, Pallas kernels for 0%

profile of v1, /device:TPU:1, one launch (start us, length us, event | category | flops | bytes accessed | tf_op | source)
XLA Modules:
  0.0 386.6 jit_solution(2916420904119000058)
XLA Ops:
  0.0 6.0 %fusion.16 = bf16[512,512]{1,0:T(8,128)(2,1)S(1)} fusion(bf16[1,512,4096]{2,1,0:T(8,128)(2,1)} %param.6), kind=kOutput, calls=%fused_computation.26 | convolution fusion | flops 2147745792 | bytes 4718592 | tf_op jit(solution)/shard_map/dot_general | solution.py:92
  6.0 1.3 fusion.19
  7.3 5.9 %fusion = f32[4096,256]{0,1:T(8,128)} fusion(bf16[1,512,4096]{2,1,0:T(8,128)(2,1)} %param.5, bf16[512,512]{1,0:T(8,128)(2,1)S(1)} %fusion.16, bf16[512,256]{1,0:T(8,128)(2,1)S(1)} %fusion.19), kind=kOutput, calls=%fused_computation.5 | convolution fusion | flops 1209139200 | bytes 9175040 | tf_op jit(solution)/shard_map/dot_general | solution.py:99
  13.2 6.6 %reshape_reshape.6 = f32[16,2,128,256]{2,1,0,3:T(2,128)} reshape(f32[4096,256]{0,1:T(8,128)} %fusion) | data formatting | bytes 8388608 | tf_op jit(solution)/shard_map/reshape;reshape | solution.py:35
  19.8 4.5 %copy.44 = f32[16,2,128,256]{2,0,3,1:T(8,128)} copy(f32[16,2,128,256]{2,1,0,3:T(2,128)} %reshape_reshape.6) | data formatting | bytes 8388608 | tf_op jit(solution)/shard_map/reshape;reshape | solution.py:35
  24.3 8.8 %all-to-all-start.1 = ((f32[2,16,128,256]{2,1,3,0:T(8,128)}), f32[2,16,128,256]{2,1,3,0:T(8,128)}, u32[]{:S(2)}, u32[]{:S(2)}) async-start(f32[2,16,128,256]{2,1,3,0:T(8,128)} %bitcast.166), calls=%async_computation.1 | async-start | bytes 8388608 | tf_op jit(solution)/shard_map/all_to_all | solution.py:41
  33.1 4.1 %all-to-all-done.1 = f32[2,16,128,256]{2,1,3,0:T(8,128)} async-done(((f32[2,16,128,256]{2,1,3,0:T(8,128)}), f32[2,16,128,256]{2,1,3,0:T(8,128)}, u32[]{:S(2)}, u32[]{:S(2)}) %all-to-all-start.1) | async-done | bytes 4194336 | tf_op jit(solution)/shard_map/all_to_all | solution.py:41
  37.2 2.7 reduce_sum.27
  39.9 0.7 copy.21
  40.6 54.2 %all_to_all.47 = f32[16,128,256]{1,2,0:T(8,128)S(1)} all-to-all(f32[16,128,256]{1,2,0:T(8,128)S(1)} %copy.21), channel_id=1, replica_groups=mesh['dp_0'=2,'dp_1'=8,'dp_2'=2,'blk'=8] {'dp_0','dp_1'}, dimensions={0} | all-to-all | bytes 4194304 | tf_op jit(solution)/shard_map/all_to_all | solution.py:49
  95.1 1.6 broadcast_in_dim.8
  96.6 7.1 %all-to-all-start.3 = ((f32[16,128,256]{2,1,0:T(8,128)}), f32[16,128,256]{2,1,0:T(8,128)S(1)}, u32[]{:S(2)}, u32[]{:S(2)}) async-start(f32[16,128,256]{2,1,0:T(8,128)} %broadcast_in_dim.8), calls=%async_computation.3 | async-start | bytes 4194304 | tf_op jit(solution)/shard_map/all_to_all | solution.py:17
  103.7 47.7 %all-to-all-done.3 = f32[16,128,256]{2,1,0:T(8,128)S(1)} async-done(((f32[16,128,256]{2,1,0:T(8,128)}), f32[16,128,256]{2,1,0:T(8,128)S(1)}, u32[]{:S(2)}, u32[]{:S(2)}) %all-to-all-start.3) | async-done | bytes 2097184 | tf_op jit(solution)/shard_map/all_to_all | solution.py:17
  151.4 0.5 broadcast_in_dim.10
  151.9 8.8 %all_to_all.44 = f32[2,16,128,256]{3,2,1,0:T(8,128)S(1)} all-to-all(f32[2,16,128,256]{3,2,1,0:T(8,128)S(1)} %broadcast_in_dim.10), channel_id=1, replica_groups=mesh['dp_0'=2,'dp_1'=8,'dp_2'=2,'blk'=8] {'dp_2'}, dimensions={0} | all-to-all | bytes 8388608 | tf_op jit(solution)/shard_map/all_to_all | solution.py:17
  160.7 1.9 copy-done.2
  162.6 6.8 %fusion.28 = f32[256,256]{1,0:T(8,128)S(1)} fusion(f32[2,16,128,256]{3,2,1,0:T(8,128)S(1)} %all_to_all.44), kind=kOutput, calls=%fused_computation.32 | convolution fusion | flops 3221225472 | bytes 4456448 | tf_op jit(solution)/shard_map/dot_general | solution.py:73
  169.6 11.7 %cholesky.130 = f32[128,128]{1,0:T(8,128)S(1)} custom-call(f32[128,128]{1,0:T(8,128)S(1)} %cholesky.194), custom_call_target="Cholesky" | custom-call | tf_op jit(solution)/shard_map/jit(cholesky)/cholesky | solution.py:79
  181.4 10.0 %custom-call.19 = f32[1,128,128]{1,2,0:T(8,128)S(1)} custom-call(f32[1,128,128]{2,1,0:T(8,128)S(1)} %get-tuple-element.49), custom_call_target="InvertDiagBlocksLowerTriangular" | custom-call | tf_op jit(solution)/shard_map/jit(cholesky)/cholesky | solution.py:79
  191.6 0.3 convolution_subtract_fusion.5
  191.9 11.7 %cholesky.147 = f32[128,128]{1,0:T(8,128)S(1)} custom-call(f32[128,128]{1,0:T(8,128)S(1)} %convolution_subtract_fusion.5), custom_call_target="Cholesky" | custom-call | tf_op jit(solution)/shard_map/jit(cholesky)/cholesky | solution.py:79
  203.6 0.7 compare_reduce_fusion.2
  205.8 4.1 %while.2 = (s32[]{:T(128)}, f32[256,256]{1,0:T(8,128)S(1)}, s32[2,2]{1,0:T(2,128)S(1)}, f32[2,128,128]{2,1,0:T(8,128)S(1)}, s32[]{:T(128)}) while((s32[]{:T(128)}, f32[256,256]{1,0:T(8,128)S(1)}, s32[2,2]{1,0:T(2,128)S(1)}, f32[2,128,128]{2,1,0:T(8,128)S(1)}, s32[]{:T(128)}) %tuple.42), condition=%wide.while_cond, body=%wide.while_body.sunk | while | flops 2 | bytes 131181 | solution.py:80
  205.8 0.6 fusion.92
  206.4 1.4 bitcast_dynamic-update-slice_fusion.4
  207.8 0.6 fusion.92
  208.5 1.4 bitcast_dynamic-update-slice_fusion.4
  209.9 20.1 %custom-call.16 = f32[2,128,128]{1,2,0:T(8,128)S(1)} custom-call(f32[2,128,128]{2,1,0:T(8,128)S(1)} %get-tuple-element.13), custom_call_target="InvertDiagBlocksLowerTriangular" | custom-call | tf_op jit(solution)/shard_map/triangular_solve | solution.py:80
  230.0 2.5 copy.24
  232.5 2.0 fusion.69
  234.6 3.5 convolution_subtract_fusion.1
  238.1 2.0 convolution_convert_fusion
  240.2 1.0 copy-done.5
  241.1 1.3 fusion.24
  242.4 0.6 fusion.34
  243.0 17.9 %all_to_all.45 = f32[32,8,256]{2,1,0:T(8,128)S(1)} all-to-all(f32[32,8,256]{2,1,0:T(8,128)S(1)} %fusion.34), channel_id=1, replica_groups=mesh['dp_0'=2,'dp_1'=8,'dp_2'=2,'blk'=8] {'dp_0','dp_1','dp_2'}, dimensions={0} | all-to-all | bytes 524288 | tf_op jit(solution)/shard_map/all_to_all | solution.py:41
  260.9 6.4 %all-to-all-start = ((bf16[8,512,128]{2,1,0:T(8,128)(2,1)}), bf16[8,512,128]{2,1,0:T(8,128)(2,1)S(1)}, u32[]{:S(2)}, u32[]{:S(2)}) async-start(bf16[8,512,128]{2,1,0:T(8,128)(2,1)} %param.8), calls=%async_computation | async-start | bytes 2097152 | tf_op jit(solution)/shard_map/all_to_all | solution.py:121
  267.3 15.1 %all-to-all-done = bf16[8,512,128]{2,1,0:T(8,128)(2,1)S(1)} async-done(((bf16[8,512,128]{2,1,0:T(8,128)(2,1)}), bf16[8,512,128]{2,1,0:T(8,128)(2,1)S(1)}, u32[]{:S(2)}, u32[]{:S(2)}) %all-to-all-start) | async-done | bytes 1048608 | tf_op jit(solution)/shard_map/all_to_all | solution.py:121
  282.5 0.8 broadcast_in_dim.11
  283.2 6.8 %all-to-all-start.6 = ((f32[32,8,256]{2,1,0:T(8,128)}), f32[32,8,256]{2,1,0:T(8,128)S(1)}, u32[]{:S(2)}, u32[]{:S(2)}) async-start(f32[32,8,256]{2,1,0:T(8,128)} %broadcast_in_dim.11), calls=%async_computation.6 | async-start | bytes 524288 | tf_op jit(solution)/shard_map/all_to_all | solution.py:17
  290.1 1.9 fusion.35
  292.0 10.0 %all-to-all-done.6 = f32[32,8,256]{2,1,0:T(8,128)S(1)} async-done(((f32[32,8,256]{2,1,0:T(8,128)}), f32[32,8,256]{2,1,0:T(8,128)S(1)}, u32[]{:S(2)}, u32[]{:S(2)}) %all-to-all-start.6) | async-done | bytes 262176 | tf_op jit(solution)/shard_map/all_to_all | solution.py:17
  302.3 11.7 %cholesky.164 = f32[128,128]{1,0:T(8,128)S(1)} custom-call(f32[128,128]{1,0:T(8,128)S(1)} %cholesky.197), custom_call_target="Cholesky" | custom-call | tf_op jit(solution)/shard_map/jit(cholesky)/cholesky | solution.py:116
  314.1 9.8 %custom-call.20 = f32[1,128,128]{1,2,0:T(8,128)S(1)} custom-call(f32[1,128,128]{2,1,0:T(8,128)S(1)} %get-tuple-element.45), custom_call_target="InvertDiagBlocksLowerTriangular" | custom-call | tf_op jit(solution)/shard_map/jit(cholesky)/cholesky | solution.py:116
  324.1 0.3 convolution_subtract_fusion.4
  324.4 11.7 %cholesky.181 = f32[128,128]{1,0:T(8,128)S(1)} custom-call(f32[128,128]{1,0:T(8,128)S(1)} %convolution_subtract_fusion.4), custom_call_target="Cholesky" | custom-call | tf_op jit(solution)/shard_map/jit(cholesky)/cholesky | solution.py:116
  336.1 0.7 compare_reduce_fusion
  336.8 0.6 compare_reduce_fusion.1
  338.7 3.9 %while.3 = (s32[]{:T(128)}, f32[256,256]{1,0:T(8,128)S(1)}, s32[2,2]{1,0:T(2,128)S(1)}, f32[2,128,128]{2,1,0:T(8,128)S(1)}, s32[]{:T(128)}) while((s32[]{:T(128)}, f32[256,256]{1,0:T(8,128)S(1)}, s32[2,2]{1,0:T(2,128)S(1)}, f32[2,128,128]{2,1,0:T(8,128)S(1)}, s32[]{:T(128)}) %tuple.48), condition=%wide.while_cond.1, body=%wide.while_body.1.sunk | while | flops 2 | bytes 131181 | solution.py:118
  338.8 0.6 fusion.93
  339.4 1.3 bitcast_dynamic-update-slice_fusion.5
  340.7 0.6 fusion.93
  341.3 1.3 bitcast_dynamic-update-slice_fusion.5
  342.6 19.9 %custom-call.17 = f32[2,128,128]{1,2,0:T(8,128)S(1)} custom-call(f32[2,128,128]{2,1,0:T(8,128)S(1)} %get-tuple-element.21), custom_call_target="InvertDiagBlocksLowerTriangular" | custom-call | tf_op jit(solution)/shard_map/triangular_solve | solution.py:118
  362.5 0.3 fusion.49
  362.8 0.3 convolution_subtract_fusion.3
  363.1 0.3 fusion.59
  363.4 0.3 fusion.58
  363.7 0.3 convolution_subtract_fusion.2
  364.0 0.3 fusion.57
  364.3 0.4 convolution_convert_fusion.3
  364.7 2.5 fusion.2
  367.4 18.1 %all_to_all.46 = bf16[8,1,512,128]{3,2,1,0:T(8,128)(2,1)S(1)} all-to-all(bf16[8,1,512,128]{3,2,1,0:T(8,128)(2,1)S(1)} %fusion.41), channel_id=1, replica_groups=mesh['dp_0'=2,'dp_1'=8,'dp_2'=2,'blk'=8] {'blk'}, dimensions={0} | all-to-all | bytes 2097152 | tf_op jit(solution)/shard_map/all_to_all | solution.py:130
  385.4 1.0 copy.78
  (55 shorter events, 1.7 us)
Async XLA Ops:
  0.0 6.0 %copy-start = (bf16[1,4096,256]{2,1,0:T(8,128)(2,1)S(1)}, bf16[1,4096,256]{2,1,0:T(8,128)(2,1)}, u32[]{:S(2)}) copy-start(bf16[1,4096,256]{2,1,0:T(8,128)(2,1)} %param.7) | copy-start | bytes 6291460
  0.0 6.0 %copy-start.3 = (bf16[1,512,4096]{2,1,0:T(8,128)(2,1)S(1)}, bf16[1,512,4096]{2,1,0:T(8,128)(2,1)}, u32[]{:S(2)}) copy-start(bf16[1,512,4096]{2,1,0:T(8,128)(2,1)} %param.5) | copy-start | bytes 12582916
  24.3 13.0 %all-to-all-start.1 = ((f32[2,16,128,256]{2,1,3,0:T(8,128)}), f32[2,16,128,256]{2,1,3,0:T(8,128)}, u32[]{:S(2)}, u32[]{:S(2)}) async-start(f32[2,16,128,256]{2,1,3,0:T(8,128)} %bitcast.166), calls=%async_computation.1 | async-start | bytes 8388608 | tf_op jit(solution)/shard_map/all_to_all | solution.py:41
  96.6 54.8 %all-to-all-start.3 = ((f32[16,128,256]{2,1,0:T(8,128)}), f32[16,128,256]{2,1,0:T(8,128)S(1)}, u32[]{:S(2)}, u32[]{:S(2)}) async-start(f32[16,128,256]{2,1,0:T(8,128)} %broadcast_in_dim.8), calls=%async_computation.3 | async-start | bytes 4194304 | tf_op jit(solution)/shard_map/all_to_all | solution.py:17
  160.7 1.9 copy-start.2
  234.5 5.6 %copy-start.9 = (bf16[4096,128]{0,1:T(8,128)(2,1)}, bf16[4096,128]{0,1:T(8,128)(2,1)S(1)}, u32[]{:S(2)}) copy-start(bf16[4096,128]{0,1:T(8,128)(2,1)S(1)} %get-tuple-element.52) | copy-start | bytes 3145732
  234.5 6.6 %copy-start.4 = (bf16[1,512,4096]{2,1,0:T(8,128)(2,1)S(1)}, bf16[1,512,4096]{2,1,0:T(8,128)(2,1)}, u32[]{:S(2)}) copy-start(bf16[1,512,4096]{2,1,0:T(8,128)(2,1)} %param.5) | copy-start | bytes 12582916
  240.1 1.0 copy-start.5
  242.4 47.6 %copy-start.6 = (bf16[4096,128]{0,1:T(8,128)(2,1)S(1)}, bf16[4096,128]{0,1:T(8,128)(2,1)}, u32[]{:S(2)}) copy-start(bf16[4096,128]{0,1:T(8,128)(2,1)} %copy-done.5) | copy-start | bytes 3145732
  260.9 21.5 %all-to-all-start = ((bf16[8,512,128]{2,1,0:T(8,128)(2,1)}), bf16[8,512,128]{2,1,0:T(8,128)(2,1)S(1)}, u32[]{:S(2)}, u32[]{:S(2)}) async-start(bf16[8,512,128]{2,1,0:T(8,128)(2,1)} %param.8), calls=%async_computation | async-start | bytes 2097152 | tf_op jit(solution)/shard_map/all_to_all | solution.py:121
  282.5 7.6 %copy-start.8 = (bf16[8,512,128]{2,1,0:T(8,128)(2,1)}, bf16[8,512,128]{2,1,0:T(8,128)(2,1)S(1)}, u32[]{:S(2)}) copy-start(bf16[8,512,128]{2,1,0:T(8,128)(2,1)S(1)} %all-to-all-done) | copy-start | bytes 3145732
  283.2 18.7 %all-to-all-start.6 = ((f32[32,8,256]{2,1,0:T(8,128)}), f32[32,8,256]{2,1,0:T(8,128)S(1)}, u32[]{:S(2)}, u32[]{:S(2)}) async-start(f32[32,8,256]{2,1,0:T(8,128)} %broadcast_in_dim.11), calls=%async_computation.6 | async-start | bytes 524288 | tf_op jit(solution)/shard_map/all_to_all | solution.py:17
  292.0 72.7 %copy-start.7 = (bf16[4096,128]{0,1:T(8,128)(2,1)S(1)}, bf16[4096,128]{0,1:T(8,128)(2,1)}, u32[]{:S(2)}) copy-start(bf16[4096,128]{0,1:T(8,128)(2,1)} %copy-done.5) | copy-start | bytes 3145732
  364.7 21.7 %copy-start.1 = (bf16[1,4096,256]{2,1,0:T(8,128)(2,1)S(1)}, bf16[1,4096,256]{2,1,0:T(8,128)(2,1)}, u32[]{:S(2)}) copy-start(bf16[1,4096,256]{2,1,0:T(8,128)(2,1)} %param.7) | copy-start | bytes 6291460
